TPU v7x, 256 devices: a whole 4x4x8 slice. The times are simulated.
256 devices in a mesh: blk: 32 (over z, x_lo, core), col: 8 (over x_hi, y).
Axes of the slice: x: 4 (x_hi: 2, x_lo: 2; x = x_hi * 2 + x_lo), y: 4, z: 8, core: 2. Of those that a mesh axis runs over, the one named last changes fastest.
Arguments:
- feat1: bfloat16 [128, 384, 256], P('blk', 'col'), may hold values from -40 to 40
- feat2: bfloat16 [128, 384, 256], P('blk', 'col'), may hold values from -40 to 40
Outputs:
- flow: float32 [2, 128, 384], P(None, 'blk', 'col')
- grad_flow: float32 [2, 128, 384], P(None, 'blk', 'col')
- grad_warped: float32 [128, 384, 256], P('blk', 'col')
All inputs are finite; a program needn't handle non-finite values.
Results may differ from a plain program's by a relative error of at most 0.0075.
Values may be sent and summed in bfloat16 or wider, within the bound.
No kernel may reach another device: no remote copies, remote signals or barrier semaphores. Data moves between devices by JAX's collectives and lax.ppermute only.
A program may use at most 64 MiB of HBM per device.

v0:
```python
import math
import jax
import jax.numpy as jnp
from jax import lax
from jax.sharding import PartitionSpec as P

ssim_one = 0.01
ssim_two = 0.03
charb_sq = 0.0001


def with_halo(value, sides, width):
    for axis, dim in sides:
        count, length = (lax.axis_size(axis), value.shape[dim])
        up = [(i, (i + 1) % count) for i in range(count - 1)]
        down = [(j, i) for i, j in up]
        last = lax.slice_in_dim(value, length - width, length, axis=dim)
        first = lax.slice_in_dim(value, 0, width, axis=dim)
        before = lax.ppermute(last, axis, up)
        after = lax.ppermute(first, axis, down)
        value = jnp.concatenate([before, value, after], axis=dim)
    return value


def box_valid(padded):
    rows_out = padded.shape[0] - 2
    cols_out = padded.shape[1] - 2
    total = jnp.zeros((rows_out, cols_out) + padded.shape[2:], padded.dtype)
    for offset_r in range(3):
        for offset_c in range(3):
            total = total + padded[offset_r : offset_r + rows_out, offset_c : offset_c + cols_out]
    return total / 9.0


def ssim_loss(mean_y, var_y, cov_xy, mean_x, var_x):
    top = (2.0 * mean_x * mean_y + ssim_one) * (2.0 * cov_xy + ssim_two)
    bottom = (mean_x * mean_x + mean_y * mean_y + ssim_one) * (var_x + var_y + ssim_two)
    return jnp.sum((1.0 - top / bottom) * 0.5)


def local_terms(xpad, ypad):
    mean_x = box_valid(xpad)
    mean_y = box_valid(ypad)
    var_x = box_valid(xpad * xpad) - mean_x * mean_x
    var_y = box_valid(ypad * ypad) - mean_y * mean_y
    cov_xy = box_valid(xpad * ypad) - mean_x * mean_y
    loss, pull = jax.vjp(
        lambda one, two, three: ssim_loss(one, two, three, mean_x, var_x), mean_y, var_y, cov_xy
    )
    grad_mean, grad_var, grad_cov = pull(jnp.ones_like(loss))
    first = grad_mean - 2.0 * grad_var * mean_y - grad_cov * mean_x
    return (first, grad_var, grad_cov)


def edge_weight(lower, upper):
    return jnp.exp(-jnp.mean(jnp.abs(upper - lower), axis=-1))


def charbonnier(weight, delta):
    return weight * delta / jnp.sqrt(delta * delta + charb_sq)


def absorb(carry, queries, keys, key_y, key_x, scale):
    total_keys = keys.shape[0]
    width = keys.shape[1]
    step = min(total_keys, 2048)
    while total_keys % step != 0:
        step = step - 1
    blocks = total_keys // step

    def visit(state, item):
        top, total, acc, along_y, along_x = state
        key_block, block_y, block_x = item
        score = (
            lax.dot_general(
                queries, key_block, (((1,), (1,)), ((), ())), preferred_element_type=jnp.float32
            )
            * scale
        )
        new_top = jnp.maximum(top, jnp.max(score, axis=1))
        shrink = jnp.exp(top - new_top)
        expo = jnp.exp(score - new_top[:, None])
        total = total * shrink + jnp.sum(expo, axis=1)
        acc = acc * shrink[:, None] + jnp.dot(
            expo.astype(jnp.bfloat16), key_block, preferred_element_type=jnp.float32
        )
        along_y = along_y * shrink + jnp.sum(expo * block_y[None, :], axis=1)
        along_x = along_x * shrink + jnp.sum(expo * block_x[None, :], axis=1)
        return ((new_top, total, acc, along_y, along_x), None)

    items = (
        keys.reshape(blocks, step, width),
        key_y.reshape(blocks, step),
        key_x.reshape(blocks, step),
    )
    carry, unused = lax.scan(visit, carry, items)
    return carry


def body(feat1, feat2):
    rows, cols, width = feat1.shape
    ncol = lax.axis_size("col")
    full_rows = rows * lax.axis_size("blk")
    full_cols = cols * ncol
    row_start = lax.axis_index("blk") * rows
    col_start = lax.axis_index("col") * cols
    scale = 1.0 / math.sqrt(width)
    tokens = rows * cols
    queries = feat1.reshape(tokens, width)
    init = (
        jnp.full((tokens,), -1e30, jnp.float32),
        jnp.zeros((tokens,), jnp.float32),
        jnp.zeros((tokens, width), jnp.float32),
        jnp.zeros((tokens,), jnp.float32),
        jnp.zeros((tokens,), jnp.float32),
    )

    def norm_y(index):
        return (index.astype(jnp.float32) + 0.5) * (2.0 / full_rows) - 1.0

    def norm_x(index):
        return (index.astype(jnp.float32) + 0.5) * (2.0 / full_cols) - 1.0

    piece = lax.all_gather(feat2, ("blk", "col"), axis=0, tiled=True)
    count = piece.shape[0]
    gathered = jnp.arange(count, dtype=jnp.int32)
    shard = gathered // rows
    tile_y = shard // ncol * rows + gathered % rows
    tile_x = shard % ncol * cols
    grid_y = jnp.broadcast_to(tile_y[:, None], (count, cols))
    grid_x = tile_x[:, None] + jnp.arange(cols, dtype=jnp.int32)[None, :]
    carry = absorb(
        init,
        queries,
        piece.reshape(count * cols, width),
        norm_y(grid_y).reshape(-1),
        norm_x(grid_x).reshape(-1),
        scale,
    )
    top, total, acc, along_y, along_x = carry
    warped = (acc / total[:, None]).astype(jnp.bfloat16).reshape(rows, cols, width)
    own_y = norm_y(row_start + jnp.arange(rows, dtype=jnp.int32))
    own_x = norm_x(col_start + jnp.arange(cols, dtype=jnp.int32))
    flow = jnp.stack(
        [
            (along_y / total).reshape(rows, cols) - own_y[:, None],
            (along_x / total).reshape(rows, cols) - own_x[None, :],
        ]
    )
    pair = jnp.stack([feat1, warped])
    xval = feat1.astype(jnp.float32)
    yval = warped.astype(jnp.float32)
    margin = 1
    padded = with_halo(pair, (("blk", 1), ("col", 2)), 1)
    xpad = padded[0].astype(jnp.float32)
    ypad = padded[1].astype(jnp.float32)
    first, grad_var, grad_cov = local_terms(xpad, ypad)
    maps = jnp.stack([first, grad_var, grad_cov])
    beside_all = with_halo(maps.astype(jnp.bfloat16), (("blk", 1), ("col", 2)), 1).astype(
        maps.dtype
    )
    spread_first = box_valid(beside_all[0])
    spread_var = box_valid(beside_all[1])
    spread_cov = box_valid(beside_all[2])
    grad_warped = spread_first + 2.0 * yval * spread_var + xval * spread_cov
    flow_pad = with_halo(flow, (("blk", 1), ("col", 2)), 1)
    x_rows = xpad[margin - 1 : margin + rows + 1, margin : margin + cols]
    x_cols = xpad[margin : margin + rows, margin - 1 : margin + cols + 1]
    edge_y = row_start - 1 + jnp.arange(rows + 1, dtype=jnp.int32)
    valid_y = (edge_y >= 0) & (edge_y <= full_rows - 2)
    edge_x = col_start - 1 + jnp.arange(cols + 1, dtype=jnp.int32)
    valid_x = (edge_x >= 0) & (edge_x <= full_cols - 2)
    delta_y = flow_pad[:, 1:, 1:-1] - flow_pad[:, :-1, 1:-1]
    push_y = jnp.where(
        valid_y[None, :, None],
        charbonnier(edge_weight(x_rows[:-1], x_rows[1:])[None], delta_y),
        0.0,
    )
    delta_x = flow_pad[:, 1:-1, 1:] - flow_pad[:, 1:-1, :-1]
    push_x = jnp.where(
        valid_x[None, None, :],
        charbonnier(edge_weight(x_cols[:, :-1], x_cols[:, 1:])[None], delta_x),
        0.0,
    )
    grad_flow = push_y[:, :rows] - push_y[:, 1:] + push_x[:, :, :cols] - push_x[:, :, 1:]
    return (flow, grad_flow, grad_warped)


def solution(mesh):
    placed = (P("blk", "col", None), P("blk", "col", None))
    return jax.shard_map(
        body,
        mesh=mesh,
        in_specs=placed,
        out_specs=(P(None, "blk", "col"), P(None, "blk", "col"), P("blk", "col", None)),
        check_vma=False,
    )
```

profile of v0, /device:TPU:132, one launch (start us, length us, event | category | flops | bytes accessed | tf_op | source)
XLA Modules:
  0.0 919.5 jit_solution(4387927049897352818)
XLA Ops:
  9.2 743.5 %all-gather.2.cloned.1.call-done = bf16[1024,48,256]{2,1,0:T(8,128)(2,1)} async-done(((bf16[4,48,256]{2,1,0:T(8,128)(2,1)}), bf16[1024,48,256]{2,1,0:T(8,128)(2,1)}) %all-gather.2.cloned.1.call-update) | async-done | bytes 25165840 | tf_op jit(solution)/shard_map/all_gather | solution.py:124
  752.7 100.4 %while.19 = (s32[]{:T(128)}, f32[192]{0:T(256)S(1)}, f32[192]{0:T(256)S(1)}, f32[192,256]{1,0:T(8,128)S(1)}, f32[192]{0:T(256)S(1)}, /*index=5*/f32[192]{0:T(256...) while((s32[]{:T(128)}, f32[192]{0:T(256)S(1)}, ...), condition=%wide.region_5.6_spmd.clone, body=%wide.region_0.5_spmd.clone.sunk | while | flops 406734528 | bytes 7375766 | solution.py:96
  756.9 1.8 fusion.87
  761.1 1.8 fusion.87
  769.5 1.8 fusion.87
  773.7 1.8 fusion.87
  777.9 1.8 fusion.87
  786.2 1.8 fusion.87
  794.6 1.8 fusion.87
  798.8 1.8 fusion.87
  803.0 1.8 fusion.87
  811.3 1.8 fusion.87
  819.7 1.8 fusion.87
  823.9 1.8 fusion.87
  828.1 1.8 fusion.87
  836.4 1.8 fusion.87
  844.8 1.8 fusion.87
  853.4 4.2 collective-permute-start.4
  857.6 1.9 collective-permute-start.5
  860.3 5.7 collective-permute-start.1
  866.0 1.9 collective-permute-start
  868.0 5.5 collective-permute-done
  873.5 1.9 collective-permute-start.3
  875.5 3.9 collective-permute-start.2
  879.5 1.9 collective-permute-start.7
  881.4 7.5 collective-permute-start.6
  890.5 1.9 collective-permute-start.9
  892.4 2.4 collective-permute-start.8
  895.0 5.2 collective-permute-done.8
  900.2 1.9 collective-permute-start.11
  902.1 3.9 collective-permute-start.10
  906.7 4.7 collective-permute-done.10
  (233 shorter events, 78.4 us)
Async XLA Ops:
  7.2 745.6 %copy-start = (bf16[4,48,256]{2,1,0:T(8,128)(2,1)S(1)}, bf16[4,48,256]{2,1,0:T(8,128)(2,1)}, u32[]{:S(2)}) copy-start(bf16[4,48,256]{2,1,0:T(8,128)(2,1)} %param.4) | copy-start | bytes 294916
  7.2 745.6 %all-gather.2.cloned.1.call-start = ((), (), s32[]{:S(2)}) async-start(), calls=%async_computation | async-start | bytes 25264128 | tf_op jit(solution)/shard_map/all_gather | solution.py:124
  853.4 14.5 %collective-permute-start.4 = (f32[2,1,48]{2,1,0:T(1,128)S(1)}, f32[2,1,48]{2,1,0:T(1,128)S(1)}, u32[]{:S(2)}, u32[]{:S(2)}) collective-permute-start(f32[2,1,48]{2,1,0:T(1,128)S(1)} %get-tuple-element.154), channel_id=1, source_target_pairs={{8,0},{16,8},{24,16},{32,24},{40,32},{48,40},{56,48},{64,56},{72,6... | collective-permute-start | bytes 1160 | tf_op jit(solution)/shard_map/ppermute | solution.py:20
  857.6 10.3 %collective-permute-start.5 = (f32[2,1,48]{2,1,0:T(1,128)S(1)}, f32[2,1,48]{2,1,0:T(1,128)S(1)}, u32[]{:S(2)}, u32[]{:S(2)}) collective-permute-start(f32[2,1,48]{2,1,0:T(1,128)S(1)} %get-tuple-element.153), channel_id=1, source_target_pairs={{0,8},{8,16},{16,24},{24,32},{32,40},{40,48},{48,56},{56,64},{64,7... | collective-permute-start | bytes 1160 | tf_op jit(solution)/shard_map/ppermute | solution.py:19
  860.3 7.7 collective-permute-start.1
  866.0 7.5 collective-permute-start
  873.5 15.4 %collective-permute-start.3 = (bf16[2,6,1,256]{3,2,1,0:T(2,128)(2,1)S(1)}, bf16[2,6,1,256]{3,2,1,0:T(2,128)(2,1)S(1)}, u32[]{:S(2)}, u32[]{:S(2)}) collective-permute-start(bf16[2,6,1,256]{3,2,1,0:T(2,128)(2,1)S(1)} %get-tuple-element.148), channel_id=1, source_target_pairs={{1,0},{2,1},{3,2},{4,3},{5,4},{6,5},{7,6},{9,8},{10,9},{11,10},{12... | collective-permute-start | bytes 18440 | tf_op jit(solution)/shard_map/ppermute | solution.py:20
  875.5 13.5 %collective-permute-start.2 = (bf16[2,6,1,256]{3,2,1,0:T(2,128)(2,1)S(1)}, bf16[2,6,1,256]{3,2,1,0:T(2,128)(2,1)S(1)}, u32[]{:S(2)}, u32[]{:S(2)}) collective-permute-start(bf16[2,6,1,256]{3,2,1,0:T(2,128)(2,1)S(1)} %get-tuple-element.147), channel_id=1, source_target_pairs={{0,1},{1,2},{2,3},{3,4},{4,5},{5,6},{6,7},{8,9},{9,10},{10,11},{11... | collective-permute-start | bytes 18440 | tf_op jit(solution)/shard_map/ppermute | solution.py:19
  879.5 15.4 %collective-permute-start.7 = (f32[2,6,1]{2,1,0:T(8,128)S(1)}, f32[2,6,1]{2,1,0:T(8,128)S(1)}, u32[]{:S(2)}, u32[]{:S(2)}) collective-permute-start(f32[2,6,1]{2,1,0:T(8,128)S(1)} %get-tuple-element.152), channel_id=1, source_target_pairs={{0,1},{1,2},{2,3},{3,4},{4,5},{5,6},{6,7},{8,9},{9,10},{10,11},{11... | collective-permute-start | bytes 152 | tf_op jit(solution)/shard_map/ppermute | solution.py:19
  881.4 13.5 %collective-permute-start.6 = (f32[2,6,1]{2,1,0:T(8,128)S(1)}, f32[2,6,1]{2,1,0:T(8,128)S(1)}, u32[]{:S(2)}, u32[]{:S(2)}) collective-permute-start(f32[2,6,1]{2,1,0:T(8,128)S(1)} %get-tuple-element.151), channel_id=1, source_target_pairs={{1,0},{2,1},{3,2},{4,3},{5,4},{6,5},{7,6},{9,8},{10,9},{11,10},{12... | collective-permute-start | bytes 152 | tf_op jit(solution)/shard_map/ppermute | solution.py:20
  890.5 4.5 collective-permute-start.9
  892.4 7.8 collective-permute-start.8
  900.2 6.5 collective-permute-start.11
  902.1 9.3 %collective-permute-start.10 = (bf16[3,6,1,256]{3,2,1,0:T(2,128)(2,1)S(1)}, bf16[3,6,1,256]{3,2,1,0:T(2,128)(2,1)S(1)}, u32[]{:S(2)}, u32[]{:S(2)}) collective-permute-start(bf16[3,6,1,256]{3,2,1,0:T(2,128)(2,1)S(1)} %get-tuple-element.138), channel_id=1, source_target_pairs={{0,1},{1,2},{2,3},{3,4},{4,5},{5,6},{6,7},{8,9},{9,10},{10,11},{11... | collective-permute-start | bytes 27656 | tf_op jit(solution)/shard_map/ppermute | solution.py:19
Sparse Core Ops, SparseCore 0:
  9.9 742.8 all-gather.1
where the time goes:
time: 922 us; the launch traced here: 919 us
  waiting for transfers between devices  760 us (82%)
  matrix products  83.4 us (9%)
  starting transfers between devices  39.2 us (4%)
  other arithmetic  19.7 us (2%)
  between operations  14.4 us (2%)
    all_gather x1, waiting for transfers between devices, body(): piece = lax.all_gather(feat2, ('blk', 'col'), axis=0, tiled=True)  744 us
    dot_general x24, matrix products, visit(): lax.dot_general(queries, key_block, (((1,), (1,)), ((), ())), preferred_e...  43.6 us
    dot_general x24, matrix products, visit(): jnp.dot(expo.astype(jnp.bfloat16), key_block, preferred_element_type=jnp....  39.8 us
    ppermute x6, starting transfers between devices, with_halo(): after = lax.ppermute(first, axis, down)  23.2 us
  transfers between devices with their start and end apart: 13, of which 4 were waited for; matrix products, arithmetic and copies ran while one was open for 0% of the time, Pallas kernels for 0%

commit v1 on v0

--- a/solution.py
+++ b/solution.py
@@ -121,7 +121,10 @@
     def norm_x(index):
         return (index.astype(jnp.float32) + 0.5) * (2.0 / full_cols) - 1.0
 
-    piece = lax.all_gather(feat2, ("blk", "col"), axis=0, tiled=True)
+    piece = jnp.concatenate(
+        lax.all_to_all(jnp.stack([feat2] * lax.axis_size(("blk", "col"))), ("blk", "col"), 0, 0),
+        axis=0,
+    )
     count = piece.shape[0]
     gathered = jnp.arange(count, dtype=jnp.int32)
     shard = gathered // rows

time: 922 us -> 731 us (0.79)
  waiting for transfers between devices: 760 us -> 544 us
  starting transfers between devices: 39.2 us -> 63.9 us
  between operations: 14.4 us -> 1 us
  local copies, waits for them, and re-layouts: 1.86 us -> 11.1 us
    all_gather x1 -> x0, waiting for transfers between devices: 744 us -> none  [body(): piece = lax.all_gather(feat2, ('blk', 'col'), axis=0, tiled=True)]
    all_to_all x0 -> x1, waiting for transfers between devices: none -> 539 us  [body(): lax.all_to_all(jnp.stack([feat2] * lax.axis_size(('blk', 'col'))), ('blk'...]
    ppermute x6, waiting for transfers between devices: 15.4 us -> 0.02 us  [with_halo(): before = lax.ppermute(last, axis, up)]
    all_to_all x0 -> x1, starting transfers between devices: none -> 14.7 us  [body(): lax.all_to_all(jnp.stack([feat2] * lax.axis_size(('blk', 'col'))), ('blk'...]
    ppermute x6, starting transfers between devices: 23.2 us -> 35.8 us  [with_halo(): after = lax.ppermute(first, axis, down)]
    another operation x0 -> x1, local copies, waits for them, and re-layouts: none -> 9.26 us  [body(): jnp.stack([feat2] * lax.axis_size(('blk', 'col')))]
  transfers between devices with their start and end apart: 13 -> 13, of which waited for: 4 -> 4; matrix products, arithmetic and copies ran while one was open for 0% -> 1% of each run, Pallas kernels for 0% -> 0%
where the time goes in v1:
time: 731 us; the launch traced here: 724 us
  waiting for transfers between devices  544 us (74%)
  matrix products  83.6 us (11%)
  starting transfers between devices  63.9 us (9%)
  other arithmetic  19.6 us (3%)
  local copies, waits for them, and re-layouts  11.1 us (2%)
    all_to_all x1, waiting for transfers between devices, body(): lax.all_to_all(jnp.stack([feat2] * lax.axis_size(('blk', 'col'))), ('blk'...  539 us
    dot_general x24, matrix products, visit(): lax.dot_general(queries, key_block, (((1,), (1,)), ((), ())), preferred_e...  43.8 us
    dot_general x24, matrix products, visit(): jnp.dot(expo.astype(jnp.bfloat16), key_block, preferred_element_type=jnp....  39.8 us
    ppermute x6, starting transfers between devices, with_halo(): after = lax.ppermute(first, axis, down)  35.8 us
    all_to_all x1, starting transfers between devices, body(): lax.all_to_all(jnp.stack([feat2] * lax.axis_size(('blk', 'col'))), ('blk'...  14.7 us
  transfers between devices with their start and end apart: 13, of which 4 were waited for; matrix products, arithmetic and copies ran while one was open for 1% of the time, Pallas kernels for 0%

profile of v1, /device:TPU:132, one launch (start us, length us, event | category | flops | bytes accessed | tf_op | source)
XLA Modules:
  0.0 724.3 jit_solution(18203653512807761041)
XLA Ops:
  0.6 9.3 %stack.20 = bf16[256,4,48,256]{3,2,1,0:T(8,128)(2,1)} broadcast(bf16[4,48,256]{2,1,0:T(8,128)(2,1)} %param.5), dimensions={1,2,3} | broadcast | bytes 25264128 | tf_op jit(solution)/shard_map/stack | solution.py:125
  9.9 14.7 %all-to-all-start = ((bf16[256,4,48,256]{3,2,1,0:T(8,128)(2,1)}), bf16[256,4,48,256]{3,2,1,0:T(8,128)(2,1)}, u32[]{:S(2)}, u32[]{:S(2)}) async-start(bf16[256,4,48,256]{3,2,1,0:T(8,128)(2,1)} %stack.20), calls=%async_computation | async-start | bytes 50331648 | tf_op jit(solution)/shard_map/all_to_all | solution.py:125
  25.9 539.4 %all-to-all-done = bf16[256,4,48,256]{3,2,1,0:T(8,128)(2,1)} async-done(((bf16[256,4,48,256]{3,2,1,0:T(8,128)(2,1)}), bf16[256,4,48,256]{3,2,1,0:T(8,128)(2,1)}, u32[]{:S(2)}, u32[]{:S(2)}) %all-to-all-start) | async-done | bytes 25165856 | tf_op jit(solution)/shard_map/all_to_all | solution.py:125
  565.3 100.6 %while.19 = (s32[]{:T(128)}, f32[192]{0:T(256)S(1)}, f32[192]{0:T(256)S(1)}, f32[192,256]{1,0:T(8,128)S(1)}, f32[192]{0:T(256)S(1)}, /*index=5*/f32[192]{0:T(256...) while((s32[]{:T(128)}, f32[192]{0:T(256)S(1)}, ...), condition=%wide.region_5.6_spmd.clone, body=%wide.region_0.5_spmd.clone.sunk | while | flops 406734528 | bytes 7376774 | solution.py:96
  569.5 1.8 fusion.87
  573.7 1.8 fusion.87
  577.9 1.8 fusion.87
  582.1 1.8 fusion.87
  586.3 1.8 fusion.87
  594.7 1.8 fusion.87
  598.8 1.8 fusion.87
  603.0 1.8 fusion.87
  607.2 1.8 fusion.87
  615.6 1.8 fusion.87
  619.8 1.8 fusion.87
  624.0 1.8 fusion.87
  628.2 1.8 fusion.87
  632.4 1.8 fusion.87
  636.6 1.8 fusion.87
  640.8 1.8 fusion.87
  666.3 7.3 %collective-permute-start.4 = (f32[2,1,48]{2,1,0:T(1,128)S(1)}, f32[2,1,48]{2,1,0:T(1,128)S(1)}, u32[]{:S(2)}, u32[]{:S(2)}) collective-permute-start(f32[2,1,48]{2,1,0:T(1,128)S(1)} %get-tuple-element.154), channel_id=1, source_target_pairs={{8,0},{16,8},{24,16},{32,24},{40,32},{48,40},{56,48},{64,56},{72,6... | collective-permute-start | bytes 1160 | tf_op jit(solution)/shard_map/ppermute | solution.py:20
  673.6 1.9 collective-permute-start.5
  676.1 1.9 collective-permute-start
  678.1 5.8 collective-permute-start.1
  685.6 1.9 collective-permute-start.2
  687.5 7.5 %collective-permute-start.3 = (bf16[2,6,1,256]{3,2,1,0:T(2,128)(2,1)S(1)}, bf16[2,6,1,256]{3,2,1,0:T(2,128)(2,1)S(1)}, u32[]{:S(2)}, u32[]{:S(2)}) collective-permute-start(bf16[2,6,1,256]{3,2,1,0:T(2,128)(2,1)S(1)} %get-tuple-element.148), channel_id=1, source_target_pairs={{1,0},{2,1},{3,2},{4,3},{5,4},{6,5},{7,6},{9,8},{10,9},{11,10},{12... | collective-permute-start | bytes 18440 | tf_op jit(solution)/shard_map/ppermute | solution.py:20
  695.1 1.9 collective-permute-start.6
  697.0 3.9 collective-permute-start.7
  702.5 1.9 collective-permute-start.8
  704.4 5.8 collective-permute-start.9
  712.1 1.9 collective-permute-start.10
  714.1 7.5 %collective-permute-start.11 = (bf16[3,6,1,256]{3,2,1,0:T(2,128)(2,1)S(1)}, bf16[3,6,1,256]{3,2,1,0:T(2,128)(2,1)S(1)}, u32[]{:S(2)}, u32[]{:S(2)}) collective-permute-start(bf16[3,6,1,256]{3,2,1,0:T(2,128)(2,1)S(1)} %get-tuple-element.139), channel_id=1, source_target_pairs={{1,0},{2,1},{3,2},{4,3},{5,4},{6,5},{7,6},{9,8},{10,9},{11,10},{12... | collective-permute-start | bytes 27656 | tf_op jit(solution)/shard_map/ppermute | solution.py:20
  (233 shorter events, 80.2 us)
Async XLA Ops:
  9.9 555.4 %all-to-all-start = ((bf16[256,4,48,256]{3,2,1,0:T(8,128)(2,1)}), bf16[256,4,48,256]{3,2,1,0:T(8,128)(2,1)}, u32[]{:S(2)}, u32[]{:S(2)}) async-start(bf16[256,4,48,256]{3,2,1,0:T(8,128)(2,1)} %stack.20), calls=%async_computation | async-start | bytes 50331648 | tf_op jit(solution)/shard_map/all_to_all | solution.py:125
  24.6 540.7 %copy-start = (bf16[4,48,256]{2,1,0:T(8,128)(2,1)S(1)}, bf16[4,48,256]{2,1,0:T(8,128)(2,1)}, u32[]{:S(2)}) copy-start(bf16[4,48,256]{2,1,0:T(8,128)(2,1)} %param.4) | copy-start | bytes 294916
  666.3 17.5 %collective-permute-start.4 = (f32[2,1,48]{2,1,0:T(1,128)S(1)}, f32[2,1,48]{2,1,0:T(1,128)S(1)}, u32[]{:S(2)}, u32[]{:S(2)}) collective-permute-start(f32[2,1,48]{2,1,0:T(1,128)S(1)} %get-tuple-element.154), channel_id=1, source_target_pairs={{8,0},{16,8},{24,16},{32,24},{40,32},{48,40},{56,48},{64,56},{72,6... | collective-permute-start | bytes 1160 | tf_op jit(solution)/shard_map/ppermute | solution.py:20
  673.6 10.2 %collective-permute-start.5 = (f32[2,1,48]{2,1,0:T(1,128)S(1)}, f32[2,1,48]{2,1,0:T(1,128)S(1)}, u32[]{:S(2)}, u32[]{:S(2)}) collective-permute-start(f32[2,1,48]{2,1,0:T(1,128)S(1)} %get-tuple-element.153), channel_id=1, source_target_pairs={{0,8},{8,16},{16,24},{24,32},{32,40},{40,48},{48,56},{56,64},{64,7... | collective-permute-start | bytes 1160 | tf_op jit(solution)/shard_map/ppermute | solution.py:19
  676.1 7.7 %collective-permute-start = (bf16[2,1,48,256]{3,2,1,0:T(8,128)(2,1)S(1)}, bf16[2,1,48,256]{3,2,1,0:T(8,128)(2,1)S(1)}, u32[]{:S(2)}, u32[]{:S(2)}) collective-permute-start(bf16[2,1,48,256]{3,2,1,0:T(8,128)(2,1)S(1)} %get-tuple-element.149), channel_id=1, source_target_pairs={{0,8},{8,16},{16,24},{24,32},{32,40},{40,48},{48,56},{56,64},{64,7... | collective-permute-start | bytes 147464 | tf_op jit(solution)/shard_map/ppermute | solution.py:19
  678.1 7.5 %collective-permute-start.1 = (bf16[2,1,48,256]{3,2,1,0:T(8,128)(2,1)S(1)}, bf16[2,1,48,256]{3,2,1,0:T(8,128)(2,1)S(1)}, u32[]{:S(2)}, u32[]{:S(2)}) collective-permute-start(bf16[2,1,48,256]{3,2,1,0:T(8,128)(2,1)S(1)} %get-tuple-element.150), channel_id=1, source_target_pairs={{8,0},{16,8},{24,16},{32,24},{40,32},{48,40},{56,48},{64,56},{72,6... | collective-permute-start | bytes 147464 | tf_op jit(solution)/shard_map/ppermute | solution.py:20
  685.6 15.4 %collective-permute-start.2 = (bf16[2,6,1,256]{3,2,1,0:T(2,128)(2,1)S(1)}, bf16[2,6,1,256]{3,2,1,0:T(2,128)(2,1)S(1)}, u32[]{:S(2)}, u32[]{:S(2)}) collective-permute-start(bf16[2,6,1,256]{3,2,1,0:T(2,128)(2,1)S(1)} %get-tuple-element.147), channel_id=1, source_target_pairs={{0,1},{1,2},{2,3},{3,4},{4,5},{5,6},{6,7},{8,9},{9,10},{10,11},{11... | collective-permute-start | bytes 18440 | tf_op jit(solution)/shard_map/ppermute | solution.py:19
  687.5 13.5 %collective-permute-start.3 = (bf16[2,6,1,256]{3,2,1,0:T(2,128)(2,1)S(1)}, bf16[2,6,1,256]{3,2,1,0:T(2,128)(2,1)S(1)}, u32[]{:S(2)}, u32[]{:S(2)}) collective-permute-start(bf16[2,6,1,256]{3,2,1,0:T(2,128)(2,1)S(1)} %get-tuple-element.148), channel_id=1, source_target_pairs={{1,0},{2,1},{3,2},{4,3},{5,4},{6,5},{7,6},{9,8},{10,9},{11,10},{12... | collective-permute-start | bytes 18440 | tf_op jit(solution)/shard_map/ppermute | solution.py:20
  695.1 15.1 %collective-permute-start.6 = (f32[2,6,1]{2,1,0:T(8,128)S(1)}, f32[2,6,1]{2,1,0:T(8,128)S(1)}, u32[]{:S(2)}, u32[]{:S(2)}) collective-permute-start(f32[2,6,1]{2,1,0:T(8,128)S(1)} %get-tuple-element.151), channel_id=1, source_target_pairs={{1,0},{2,1},{3,2},{4,3},{5,4},{6,5},{7,6},{9,8},{10,9},{11,10},{12... | collective-permute-start | bytes 152 | tf_op jit(solution)/shard_map/ppermute | solution.py:20
  697.0 13.2 %collective-permute-start.7 = (f32[2,6,1]{2,1,0:T(8,128)S(1)}, f32[2,6,1]{2,1,0:T(8,128)S(1)}, u32[]{:S(2)}, u32[]{:S(2)}) collective-permute-start(f32[2,6,1]{2,1,0:T(8,128)S(1)} %get-tuple-element.152), channel_id=1, source_target_pairs={{0,1},{1,2},{2,3},{3,4},{4,5},{5,6},{6,7},{8,9},{9,10},{10,11},{11... | collective-permute-start | bytes 152 | tf_op jit(solution)/shard_map/ppermute | solution.py:19
  702.5 7.9 %collective-permute-start.8 = (bf16[3,1,48,256]{3,2,1,0:T(8,128)(2,1)S(1)}, bf16[3,1,48,256]{3,2,1,0:T(8,128)(2,1)S(1)}, u32[]{:S(2)}, u32[]{:S(2)}) collective-permute-start(bf16[3,1,48,256]{3,2,1,0:T(8,128)(2,1)S(1)} %get-tuple-element.145), channel_id=1, source_target_pairs={{0,8},{8,16},{16,24},{24,32},{32,40},{40,48},{48,56},{56,64},{64,7... | collective-permute-start | bytes 221192 | tf_op jit(solution)/shard_map/ppermute | solution.py:19
  704.4 7.7 %collective-permute-start.9 = (bf16[3,1,48,256]{3,2,1,0:T(8,128)(2,1)S(1)}, bf16[3,1,48,256]{3,2,1,0:T(8,128)(2,1)S(1)}, u32[]{:S(2)}, u32[]{:S(2)}) collective-permute-start(bf16[3,1,48,256]{3,2,1,0:T(8,128)(2,1)S(1)} %get-tuple-element.146), channel_id=1, source_target_pairs={{8,0},{16,8},{24,16},{32,24},{40,32},{48,40},{56,48},{64,56},{72,6... | collective-permute-start | bytes 221192 | tf_op jit(solution)/shard_map/ppermute | solution.py:20
  712.1 10.1 %collective-permute-start.10 = (bf16[3,6,1,256]{3,2,1,0:T(2,128)(2,1)S(1)}, bf16[3,6,1,256]{3,2,1,0:T(2,128)(2,1)S(1)}, u32[]{:S(2)}, u32[]{:S(2)}) collective-permute-start(bf16[3,6,1,256]{3,2,1,0:T(2,128)(2,1)S(1)} %get-tuple-element.138), channel_id=1, source_target_pairs={{0,1},{1,2},{2,3},{3,4},{4,5},{5,6},{6,7},{8,9},{9,10},{10,11},{11... | collective-permute-start | bytes 27656 | tf_op jit(solution)/shard_map/ppermute | solution.py:19
  714.1 9.0 %collective-permute-start.11 = (bf16[3,6,1,256]{3,2,1,0:T(2,128)(2,1)S(1)}, bf16[3,6,1,256]{3,2,1,0:T(2,128)(2,1)S(1)}, u32[]{:S(2)}, u32[]{:S(2)}) collective-permute-start(bf16[3,6,1,256]{3,2,1,0:T(2,128)(2,1)S(1)} %get-tuple-element.139), channel_id=1, source_target_pairs={{1,0},{2,1},{3,2},{4,3},{5,4},{6,5},{7,6},{9,8},{10,9},{11,10},{12... | collective-permute-start | bytes 27656 | tf_op jit(solution)/shard_map/ppermute | solution.py:20
